TPU v7x, 128 devices: a whole 4x4x4 slice. The times are simulated.
128 devices in a mesh: wide: 32 (over x, y, core), narrow: 4 (over z).
Axes of the slice: x: 4, y: 4, z: 4, core: 2. Of those that a mesh axis runs over, the one named last changes fastest.
Arguments:
- raw_samples: bfloat16 [1024, 32, 16384], P(('wide', 'narrow')), as said below
- filter_taps: float32 [64], replicated, may hold values from -0.75 to 0.75
- tile_pairs: int32 [16, 2], replicated, may hold values from 0 to 127, as said below
- tile_owners: int32 [16], replicated, may hold values from 0 to 3, as said below
Outputs:
- correlation_stacks: float32 [32, 64, 512], P('narrow', 'wide')
Inputs may be any that keep to these rules, and one draw needn't show every extreme that they name: `raw_samples`: noise samples, scaled per channel and per window. `tile_pairs`: each row is (source block, receiver block), and the two blocks differ. `tile_owners`: each owner has at most 8 tiles, and some owner has exactly 8.
All inputs are finite; a program needn't handle non-finite values.
Results may differ from a plain program's by a relative error of at most 0.0074.
Values may be sent and summed in bfloat16 or wider, within the bound.
No kernel may reach another device: no remote copies, remote signals or barrier semaphores. Data moves between devices by JAX's collectives and lax.ppermute only.
A program may use at most 128 MiB of HBM per device.

v0:
```python
import math
import jax
import jax.numpy as jnp
from jax import lax
from jax.sharding import PartitionSpec as P

NFFT = 4096
DECIM = 4
NBINS = 1024
SMOOTH = 63
LAGS = 512
BLK = 8
SLOTS = 8
water_level = 0.2
epsilon = 1e-06


def fir_tables(filter_taps, block_size):
    in_rows = jnp.arange(DECIM * block_size, dtype=jnp.int32)[:, None]
    out_cols = jnp.arange(block_size, dtype=jnp.int32)[None, :]
    this_index = DECIM * out_cols + DECIM - 1 - in_rows
    last_index = this_index + DECIM * block_size
    tap_count = filter_taps.shape[0]

    def taps_at(tap_index):
        inside = (tap_index >= 0) & (tap_index < tap_count)
        values = jnp.take(filter_taps, jnp.clip(tap_index, 0, tap_count - 1))
        return jnp.where(inside, values, jnp.zeros_like(values)).astype(jnp.bfloat16)

    return (taps_at(this_index), taps_at(last_index))


def decimate(samples, filter_taps):
    row_count, row_length = samples.shape
    block_size = min(128, row_length // DECIM)
    this_table, last_table = fir_tables(filter_taps, block_size)
    segments = samples.reshape(-1, DECIM * block_size)
    current = jnp.dot(segments, this_table, preferred_element_type=jnp.float32).reshape(
        row_count, -1, block_size
    )
    spilled = jnp.dot(segments, last_table, preferred_element_type=jnp.float32).reshape(
        row_count, -1, block_size
    )
    spilled = jnp.pad(spilled[:, :-1], ((0, 0), (1, 0), (0, 0)))
    return (current + spilled).reshape(row_count, -1).astype(jnp.bfloat16)


def dft_table(point_count, bin_count):
    sample_index = jnp.arange(point_count, dtype=jnp.int32)[:, None]
    frequency = 1 + jnp.arange(bin_count, dtype=jnp.int32)[None, :]
    angle = (sample_index * frequency % point_count).astype(jnp.float32) * (
        2.0 * math.pi / point_count
    )
    return jnp.concatenate([jnp.cos(angle), -jnp.sin(angle)], axis=1).astype(jnp.bfloat16)


def lag_table(point_count, bin_count, lag_count, window_count):
    frequency = 1 + jnp.arange(bin_count, dtype=jnp.int32)[:, None]
    shifted = jnp.arange(lag_count, dtype=jnp.int32)[None, :] - lag_count // 2 + point_count
    angle = (frequency * shifted % point_count).astype(jnp.float32) * (2.0 * math.pi / point_count)
    weight = 1.0 / math.sqrt(window_count * bin_count)
    return jnp.concatenate([jnp.cos(angle) * weight, -jnp.sin(angle) * weight], axis=0)


def smoother(bin_count, span_width):
    bin_index = jnp.arange(bin_count, dtype=jnp.int32)
    nearby = (jnp.abs(bin_index[:, None] - bin_index[None, :]) <= (span_width - 1) // 2).astype(
        jnp.float32
    )
    return nearby / jnp.sum(nearby, axis=0, keepdims=True)


def whiten(decimated):
    spectrum = jnp.dot(
        decimated, dft_table(decimated.shape[1], NBINS), preferred_element_type=jnp.float32
    )
    real_part = spectrum[:, :NBINS]
    imag_part = spectrum[:, NBINS:]
    magnitude = jnp.sqrt(real_part * real_part + imag_part * imag_part)
    smooth = jnp.dot(magnitude, smoother(NBINS, SMOOTH), precision=lax.Precision.HIGHEST)
    floor_level = water_level * jnp.mean(smooth, axis=1, keepdims=True) + epsilon
    factor = 1.0 / (smooth + floor_level)
    return (spectrum * jnp.concatenate([factor, factor], axis=1)).astype(jnp.bfloat16)


def block_start(block_index, chan_dev, wide_count, narrow_count):
    first_channel = block_index * BLK
    shard_index = first_channel // chan_dev
    return (
        shard_index % narrow_count * wide_count + shard_index // narrow_count
    ) * chan_dev + first_channel % chan_dev


def gather_rows(spectra, starts):

    def one_block(start_row):
        return lax.dynamic_slice_in_dim(spectra, start_row, BLK, 0)

    return jax.vmap(one_block)(starts)


def slot_cross(source, target, live_slots):
    highest = lax.Precision.HIGHEST
    src_real = source[..., :NBINS]
    src_imag = source[..., NBINS:]
    dst_real = target[..., :NBINS]
    dst_imag = target[..., NBINS:]
    real_sum = jnp.einsum("siwf,sjwf->ijsf", src_real, dst_real, precision=highest) + jnp.einsum(
        "siwf,sjwf->ijsf", src_imag, dst_imag, precision=highest
    )
    imag_sum = jnp.einsum("siwf,sjwf->ijsf", src_real, dst_imag, precision=highest) - jnp.einsum(
        "siwf,sjwf->ijsf", src_imag, dst_real, precision=highest
    )
    slot_count = source.shape[0]
    merged = jnp.concatenate(
        [
            real_sum.reshape(BLK * BLK, slot_count, NBINS),
            imag_sum.reshape(BLK * BLK, slot_count, NBINS),
        ],
        axis=2,
    )
    return merged * live_slots[None, :, None]


def stack_pairs(partial_value, window_count, wide_count):
    lag_basis = lag_table(NFFT, NBINS, LAGS, window_count)
    slot_count = partial_value.shape[1]
    pair_share = partial_value.shape[0] // wide_count
    summed = lax.psum_scatter(partial_value, "wide", scatter_dimension=0, tiled=True)
    flat = summed.reshape(pair_share * slot_count, 2 * NBINS)
    return jnp.dot(flat, lag_basis, precision=lax.Precision.HIGHEST).reshape(
        pair_share, slot_count, LAGS
    )


def on_device(raw_samples, filter_taps, tile_pairs, tile_owners):
    wide_count = lax.axis_size("wide")
    narrow_count = lax.axis_size("narrow")
    chan_dev = raw_samples.shape[0]
    window_total = raw_samples.shape[1]
    arrived = lax.all_to_all(raw_samples, "wide", split_axis=1, concat_axis=0, tiled=True)
    flat_rows = arrived.reshape(-1, arrived.shape[2])
    whitened = whiten(decimate(flat_rows, filter_taps)).reshape(
        arrived.shape[0], arrived.shape[1], 2 * NBINS
    )
    owner_index = lax.axis_index("narrow")
    slot_ids = jnp.arange(SLOTS, dtype=jnp.int32)
    owner_ids = jnp.arange(narrow_count, dtype=jnp.int32)
    owned_all = tile_owners[None, :] == owner_ids[:, None]
    rank_all = jnp.cumsum(owned_all.astype(jnp.int32), axis=1) - 1
    select_all = owned_all[:, None, :] & (rank_all[:, None, :] == slot_ids[None, :, None])
    select = lax.dynamic_index_in_dim(select_all, owner_index, 0, keepdims=False)
    pick_all = select_all.astype(jnp.int32)
    chosen_all = jnp.sum(pick_all[:, :, :, None] * tile_pairs[None, None, :, :], axis=2)
    chosen = lax.dynamic_index_in_dim(chosen_all, owner_index, 0, keepdims=False)
    live_slots = jnp.sum(select.astype(jnp.int32), axis=1).astype(jnp.float32)
    spectra = lax.all_gather(whitened, "narrow", axis=0, tiled=True)
    source = gather_rows(
        spectra, block_start(chosen[:, 0], chan_dev, wide_count, narrow_count)
    ).astype(jnp.float32)
    target = gather_rows(
        spectra, block_start(chosen[:, 1], chan_dev, wide_count, narrow_count)
    ).astype(jnp.float32)
    partial_value = slot_cross(source, target, live_slots)
    stacked = jnp.transpose(stack_pairs(partial_value, window_total, wide_count), (1, 0, 2))
    return stacked


def solution(mesh):
    in_specs = (P(("wide", "narrow"), None, None), P(), P(), P())
    out_specs = P("narrow", "wide", None)
    return jax.shard_map(
        on_device, mesh=mesh, in_specs=in_specs, out_specs=out_specs, check_vma=False
    )
```

profile of v0, /device:TPU:0, one launch (start us, length us, event | category | flops | bytes accessed | tf_op | source)
XLA Modules:
  0.0 474.6 jit_solution(13282219317979138211)
XLA Ops:
  6.5 11.2 %copy.33 = bf16[8,32,16384]{2,0,1:T(8,128)(2,1)} copy(bf16[8,32,16384]{2,1,0:T(8,128)(2,1)} %param.6) | data formatting | bytes 16777216 | tf_op args[0]
  17.7 7.7 %all-to-all-start = ((bf16[8,32,16384]{2,0,1:T(8,128)(2,1)}), bf16[8,32,16384]{2,0,1:T(8,128)(2,1)}, u32[]{:S(2)}, u32[]{:S(2)}) async-start(bf16[8,32,16384]{2,0,1:T(8,128)(2,1)} %copy.33), calls=%async_computation | async-start | bytes 16777216 | tf_op jit(solution)/shard_map/all_to_all | solution.py:141
  25.9 0.7 fusion.579
  26.6 0.7 fusion.580
  27.3 0.7 fusion.581
  28.1 0.7 fusion.582
  28.8 69.1 %cosine_convert_fusion = (bf16[4096,1024]{1,0:T(8,128)(2,1)}, bf16[4096,1024]{1,0:T(8,128)(2,1)}) fusion(s32[1024]{0:T(1024)S(1)} %iota_add_fusion), kind=kLoop, calls=%fused_computation.15 | loop fusion | flops 71303168 | bytes 16781312 | tf_op jit(solution)/shard_map/convert.24
  97.9 41.1 %all-to-all-done = bf16[8,32,16384]{2,0,1:T(8,128)(2,1)} async-done(((bf16[8,32,16384]{2,0,1:T(8,128)(2,1)}), bf16[8,32,16384]{2,0,1:T(8,128)(2,1)}, u32[]{:S(2)}, u32[]{:S(2)}) %all-to-all-start) | async-done | bytes 8388640 | tf_op jit(solution)/shard_map/all_to_all | solution.py:141
  138.9 13.5 %reshape_reshape.3 = bf16[8192,512]{1,0:T(8,128)(2,1)} reshape(bf16[32,8,1,16384]{3,1,0,2:T(8,128)(2,1)} %bitcast.65) | data formatting | bytes 16777216 | tf_op jit(solution)/shard_map/reshape;reshape | solution.py:37
  152.4 50.3 %convolution_bitcast_fusion = f32[8192,128]{0,1:T(8,128)} fusion(bf16[8192,512]{1,0:T(8,128)(2,1)} %reshape_reshape.3, bf16[]{:T(256)} %bitcast.63, bf16[]{:T(256)} %bitcast.62, bf16[]{:T(256)} %bitcast.61, bf16[]{:T(256)} %bitcast.60, bf16[]{:T(256)} %bitcast.59, bf16[]{:T(256)} %bitcast.58, bf16[]{:T(256)} %bitcast.57, bf16[]{:T(256)} %bitcast.56, ...), kind=kOutput, calls=%fused_computation.19 | convolution fusion | flops 1082916864 | bytes 12583552 | tf_op jit(solution)/shard_map/dot_general | solution.py:41
  202.7 45.8 %convolution_bitcast_fusion.1 = f32[8192,128]{0,1:T(8,128)} fusion(bf16[8192,512]{1,0:T(8,128)(2,1)S(1)} %bitcast.200, bf16[]{:T(256)} %bitcast.63, bf16[]{:T(256)} %bitcast.62, bf16[]{:T(256)} %bitcast.61, bf16[]{:T(256)} %bitcast.60, bf16[]{:T(256)} %bitcast.59, bf16[]{:T(256)} %bitcast.58, bf16[]{:T(256)} %bitcast.57, bf16[]{:T(256)} %bitcast.56, ...), kind=kOutput, calls=%fused_computation.20 | convolution fusion | flops 1082851328 | bytes 12583552 | tf_op jit(solution)/shard_map/dot_general | solution.py:38
  248.5 5.6 %copy.35 = f32[8192,128]{1,0:T(8,128)} copy(f32[8192,128]{0,1:T(8,128)} %convolution_bitcast_fusion) | data formatting | bytes 8388608 | tf_op jit(solution)/shard_map/dot_general | solution.py:41
  254.1 5.6 %copy.34 = f32[8192,128]{1,0:T(8,128)} copy(f32[8192,128]{0,1:T(8,128)} %convolution_bitcast_fusion.1) | data formatting | bytes 8388608 | tf_op jit(solution)/shard_map/dot_general | solution.py:38
  259.7 4.2 add_convert_fusion
  263.9 2.8 copy.36
  266.7 10.9 %fusion.3 = f32[256,2048]{1,0:T(8,128)S(1)} fusion(bf16[256,4096]{0,1:T(8,128)(2,1)} %bitcast.203, bf16[4096,1024]{1,0:T(8,128)(2,1)} %get-tuple-element.55, bf16[4096,1024]{1,0:T(8,128)(2,1)} %get-tuple-element.54), kind=kOutput, calls=%fused_computation.10 | convolution fusion | flops 4328521728 | bytes 20971520 | tf_op jit(solution)/shard_map/dot_general | solution.py:74
  277.6 3.8 fusion.583
  281.7 1.3 fusion.17
  283.7 57.0 %all-gather.3.cloned.1.call-done = bf16[1024,2048]{1,0:T(8,128)(2,1)} async-done(((bf16[256,2048]{1,0:T(8,128)(2,1)}), bf16[1024,2048]{1,0:T(8,128)(2,1)}) %all-gather.3.cloned.1.call-update) | async-done | bytes 4194320 | tf_op jit(solution)/shard_map/all_gather | solution.py:157
  340.7 18.2 %while.2 = (s32[]{:T(128)}, bf16[1024,1,2048]{2,0,1:T(8,128)(2,1)}, s32[8,3]{0,1:T(4,128)S(1)}, bf16[8,8,1,2048]{3,1,2,0:T(8,128)(2,1)S(1)}, s32[]{:T(128)}) while((s32[]{:T(128)}, bf16[1024,1,2048]{2,0,1:T(8,128)(2,1)}, s32[8,3]{0,1:T(4,128)S(1)}, bf16[8,8,1,2048]{3,1,2,0:T(8,128)(2,1)S(1)}, s32[]{:T(128)}) %tuple.109), condition=%wide.while_cond, body=%wide.while_body.sunk | while | flops 2 | bytes 65641 | solution.py:97
  341.0 0.6 slice.413
  341.6 1.5 bitcast_dynamic-update-slice_fusion.4
  343.3 0.6 slice.413
  343.9 1.5 bitcast_dynamic-update-slice_fusion.4
  345.5 0.6 slice.413
  346.1 1.5 bitcast_dynamic-update-slice_fusion.4
  347.8 0.6 slice.413
  348.4 1.5 bitcast_dynamic-update-slice_fusion.4
  350.0 0.6 slice.413
  350.6 1.5 bitcast_dynamic-update-slice_fusion.4
  352.8 1.5 bitcast_dynamic-update-slice_fusion.4
  355.1 1.5 bitcast_dynamic-update-slice_fusion.4
  357.3 1.5 bitcast_dynamic-update-slice_fusion.4
  359.3 17.9 %while.3 = (s32[]{:T(128)}, bf16[1024,1,2048]{2,0,1:T(8,128)(2,1)}, s32[8,3]{0,1:T(4,128)S(1)}, bf16[8,8,1,2048]{3,1,2,0:T(8,128)(2,1)S(1)}, s32[]{:T(128)}) while((s32[]{:T(128)}, bf16[1024,1,2048]{2,0,1:T(8,128)(2,1)}, s32[8,3]{0,1:T(4,128)S(1)}, bf16[8,8,1,2048]{3,1,2,0:T(8,128)(2,1)S(1)}, s32[]{:T(128)}) %tuple.110), condition=%wide.while_cond.1, body=%wide.while_body.1.sunk | while | flops 2 | bytes 65641 | solution.py:97
  360.0 1.5 bitcast_dynamic-update-slice_fusion.5
  362.2 1.5 bitcast_dynamic-update-slice_fusion.5
  363.8 0.6 slice.414
  364.4 1.5 bitcast_dynamic-update-slice_fusion.5
  366.7 1.5 bitcast_dynamic-update-slice_fusion.5
  368.9 1.5 bitcast_dynamic-update-slice_fusion.5
  371.1 1.5 bitcast_dynamic-update-slice_fusion.5
  373.4 1.5 bitcast_dynamic-update-slice_fusion.5
  375.6 1.5 bitcast_dynamic-update-slice_fusion.5
  378.1 2.6 maximum_multiply_fusion
  380.8 9.7 %cosine_multiply_fusion = (f32[1024,512]{1,0:T(8,128)S(1)}, f32[1024,512]{1,0:T(8,128)}) fusion(s32[512]{0:T(512)S(1)} %iota_add_fusion.1, s32[1024]{0:T(1024)S(1)} %iota_add_fusion), kind=kLoop, calls=%fused_computation.42 | loop fusion | flops 8912896 | bytes 4200448 | tf_op jit(solution)/shard_map/mul | solution.py:62
  390.5 72.8 %reduce-scatter.2.cloned.1.call-done = f32[2,8,2048]{2,1,0:T(8,128)} async-done(((f32[64,8,2048]{2,1,0:T(8,128)}), f32[2,8,2048]{2,1,0:T(8,128)}) %reduce-scatter.2.cloned.1.call-update) | async-done | bytes 131088 | tf_op jit(solution)/shard_map/reduce_scatter | solution.py:129
  463.3 3.8 fusion.20
  467.1 0.6 copy.41
  (67 shorter events, 9.9 us)
Async XLA Ops:
  17.7 8.1 %copy-start = (f32[64]{0:T(128)S(1)}, f32[64]{0:T(128)}, u32[]{:S(2)}) copy-start(f32[64]{0:T(128)} %param.7) | copy-start | bytes 772
  17.7 121.2 %all-to-all-start = ((bf16[8,32,16384]{2,0,1:T(8,128)(2,1)}), bf16[8,32,16384]{2,0,1:T(8,128)(2,1)}, u32[]{:S(2)}, u32[]{:S(2)}) async-start(bf16[8,32,16384]{2,0,1:T(8,128)(2,1)} %copy.33), calls=%async_computation | async-start | bytes 16777216 | tf_op jit(solution)/shard_map/all_to_all | solution.py:141
  25.4 315.2 %all-gather.3.cloned.1.call-start = ((), (), s32[]{:S(2)}) async-start(), calls=%async_computation.3 | async-start | bytes 5242880 | tf_op jit(solution)/shard_map/all_gather | solution.py:157
  152.4 50.3 %slice-start = ((s8[8388608]{0:T(1024)(128)(4,1)}), s8[4194304]{0:T(1024)(128)(4,1)S(1)}, s32[]{:S(2)}) async-start(s8[8388608]{0:T(1024)(128)(4,1)} %bitcast.199), calls=%async_computation.4 | async-start | bytes 8388608
  152.4 50.3 %slice-start.1 = ((s8[8388608]{0:T(1024)(128)(4,1)}), s8[4194304]{0:T(1024)(128)(4,1)S(1)}, s32[]{:S(2)}) async-start(s8[8388608]{0:T(1024)(128)(4,1)} %bitcast.199), calls=%async_computation.5 | async-start | bytes 8388608
  281.4 1.6 copy-start.2
  281.4 1.8 copy-start.1
  283.0 180.3 %reduce-scatter.2.cloned.1.call-start = ((), (), s32[]{:S(2)}) async-start(), calls=%async_computation.2 | async-start | bytes 4325376 | tf_op jit(solution)/shard_map/reduce_scatter | solution.py:129
Sparse Core Ops, SparseCore 0:
  283.1 57.5 all-gather.2
  380.9 82.3 reduce-scatter.1
where the time goes:
time: 477 us; the launch traced here: 475 us
  waiting for transfers between devices  171 us (36%)
  matrix products  115 us (24%)
  other arithmetic  88.6 us (19%)
  local copies, waits for them, and re-layouts  78.4 us (16%)
  between operations  13.6 us (3%)
  starting transfers between devices  7.96 us (2%)
    reduce_scatter x1, waiting for transfers between devices, stack_pairs(): lax.psum_scatter(partial_value, 'wide', scatter_dimension=0, tiled=True)  72.8 us
    another operation x3, other arithmetic  69.2 us
    all_gather x1, waiting for transfers between devices, on_device(): spectra = lax.all_gather(whitened, 'narrow', axis=0, tiled=True)  57 us
    dot_general x1, matrix products, decimate(): jnp.dot(segments, last_table, preferred_element_type=jnp.float32)  50.3 us
    dot_general x1, matrix products, decimate(): jnp.dot(segments, this_table, preferred_element_type=jnp.float32)  45.8 us
    all_to_all x1, waiting for transfers between devices, on_device(): lax.all_to_all(raw_samples, 'wide', split_axis=1, concat_axis=0, tiled=True)  41.1 us
    gather x48, local copies, waits for them, and re-layouts  35.5 us
    another operation x1, local copies, waits for them, and re-layouts, decimate(): segments = samples.reshape(-1, DECIM * block_size)  13.5 us
  transfers between devices with their start and end apart: 3, of which 3 were waited for; matrix products, arithmetic and copies ran while one was open for 17% of the time, Pallas kernels for 0%

commit v1 on v0

--- a/solution.py
+++ b/solution.py
@@ -138,7 +138,12 @@
     narrow_count = lax.axis_size("narrow")
     chan_dev = raw_samples.shape[0]
     window_total = raw_samples.shape[1]
-    arrived = lax.all_to_all(raw_samples, "wide", split_axis=1, concat_axis=0, tiled=True)
+    arrived = jnp.concatenate(
+        lax.all_to_all(
+            jnp.stack(jnp.split(raw_samples, lax.axis_size("wide"), axis=1)), "wide", 0, 0
+        ),
+        axis=0,
+    )
     flat_rows = arrived.reshape(-1, arrived.shape[2])
     whitened = whiten(decimate(flat_rows, filter_taps)).reshape(
         arrived.shape[0], arrived.shape[1], 2 * NBINS

time: 477 us -> 513 us (1.075)
  local copies, waits for them, and re-layouts: 78.4 us -> 106 us
  matrix products: 115 us -> 124 us
    slice x0 -> x1, matrix products: none -> 55.8 us  [decimate(): spilled = jnp.pad(spilled[:, :-1], ((0, 0), (1, 0), (0, 0)))]
    dot_general x1 -> x0, matrix products: 50.3 us -> none  [decimate(): jnp.dot(segments, last_table, preferred_element_type=jnp.float32)]
    unnamed x13 -> x50, local copies, waits for them, and re-layouts: 11.3 us -> 41.5 us
    split x0 -> x2, local copies, waits for them, and re-layouts: none -> 25.3 us  [on_device(): jnp.split(raw_samples, lax.axis_size('wide'), axis=1)]
    another operation x5, local copies, waits for them, and re-layouts: 14.1 us -> 1.63 us  [the longest x1 1 us: on_device(): jnp.stack(jnp.split(raw_samples, lax.axis_size('wide'), axis=1))]
    dot_general x2 -> x0, local copies, waits for them, and re-layouts: 11.2 us -> none  [the longest x1 5.61 us: decimate(): jnp.dot(segments, this_table, preferred_element_type=jnp.float32)]
  transfers between devices with their start and end apart: 3 -> 3, of which waited for: 3 -> 3; matrix products, arithmetic and copies ran while one was open for 17% -> 16% of each run, Pallas kernels for 0% -> 0%
where the time goes in v1:
time: 513 us; the launch traced here: 507 us
  waiting for transfers between devices  171 us (33%)
  matrix products  124 us (24%)
  local copies, waits for them, and re-layouts  106 us (21%)
  other arithmetic  84.6 us (16%)
  between operations  13.9 us (3%)
  starting transfers between devices  7.78 us (2%)
    reduce_scatter x1, waiting for transfers between devices, stack_pairs(): lax.psum_scatter(partial_value, 'wide', scatter_dimension=0, tiled=True)  72.8 us
    another operation x3, other arithmetic  69.4 us
    all_gather x1, waiting for transfers between devices, on_device(): spectra = lax.all_gather(whitened, 'narrow', axis=0, tiled=True)  57 us
    slice x1, matrix products, decimate(): spilled = jnp.pad(spilled[:, :-1], ((0, 0), (1, 0), (0, 0)))  55.8 us
    dot_general x1, matrix products, decimate(): jnp.dot(segments, this_table, preferred_element_type=jnp.float32)  48 us
    unnamed x50, local copies, waits for them, and re-layouts  41.5 us
    all_to_all x1, waiting for transfers between devices, on_device(): lax.all_to_all(jnp.stack(jnp.split(raw_samples, lax.axis_size('wide'), ax...  41.1 us
    gather x48, local copies, waits for them, and re-layouts  33.8 us
  transfers between devices with their start and end apart: 3, of which 3 were waited for; matrix products, arithmetic and copies ran while one was open for 16% of the time, Pallas kernels for 0%

profile of v1, /device:TPU:0, one launch (start us, length us, event | category | flops | bytes accessed | tf_op | source)
XLA Modules:
  0.0 507.4 jit_solution(3149457112491657716)
XLA Ops:
  6.5 14.1 %fusion.620 = (bf16[8,1,16384]{2,1,0:T(2,128)(2,1)S(1)}, bf16[8,1,16384]{2,1,0:T(2,128)(2,1)S(1)}, bf16[8,1,16384]{2,1,0:T(2,128)(2,1)S(1)}, bf16[8,1,16384]{2,1...) fusion(bf16[8,32,16384]{2,1,0:T(8,128)(2,1)} %param.6), kind=kLoop, calls=%fused_computation.716 | loop fusion | bytes 6815744 | tf_op jit(solution)/shard_map/split | solution.py:143
  20.7 11.2 %fusion.619 = (bf16[8,1,16384]{2,1,0:T(2,128)(2,1)S(1)}, bf16[8,1,16384]{2,1,0:T(2,128)(2,1)S(1)}, bf16[8,1,16384]{2,1,0:T(2,128)(2,1)S(1)}, bf16[8,1,16384]{2,1...) fusion(bf16[8,32,16384]{2,1,0:T(8,128)(2,1)S(1)} %copy-done), kind=kLoop, calls=%fused_computation.715 | loop fusion | bytes 9961472 | tf_op jit(solution)/shard_map/split | solution.py:143
  32.9 1.0 fusion.60
  33.9 1.0 fusion.59
  36.9 1.0 fusion.56
  38.9 1.0 fusion.54
  39.9 1.0 fusion.53
  40.9 1.0 fusion.52
  45.9 1.0 fusion.47
  46.9 1.0 fusion.46
  47.9 1.0 fusion.45
  48.9 1.0 fusion.44
  53.9 1.0 fusion.39
  55.9 1.0 fusion.37
  56.9 1.0 fusion.36
  58.9 1.0 fusion.34
  63.9 7.7 %all-to-all-start = ((bf16[32,8,1,16384]{3,1,2,0:T(8,128)(2,1)}), bf16[32,8,1,16384]{3,1,2,0:T(8,128)(2,1)}, u32[]{:S(2)}, u32[]{:S(2)}) async-start(bf16[32,8,1,16384]{3,1,2,0:T(8,128)(2,1)} %fusion.30), calls=%async_computation | async-start | bytes 16777216 | tf_op jit(solution)/shard_map/all_to_all | solution.py:142
  74.7 69.3 %cosine_convert_fusion = (bf16[4096,1024]{1,0:T(8,128)(2,1)}, bf16[4096,1024]{1,0:T(8,128)(2,1)}) fusion(s32[1024]{0:T(1024)S(1)} %iota_add_fusion), kind=kLoop, calls=%fused_computation.15 | loop fusion | flops 71303168 | bytes 16781312 | tf_op jit(solution)/shard_map/convert.24
  144.0 41.1 %all-to-all-done = bf16[32,8,1,16384]{3,1,2,0:T(8,128)(2,1)} async-done(((bf16[32,8,1,16384]{3,1,2,0:T(8,128)(2,1)}), bf16[32,8,1,16384]{3,1,2,0:T(8,128)(2,1)}, u32[]{:S(2)}, u32[]{:S(2)}) %all-to-all-start) | async-done | bytes 8388640 | tf_op jit(solution)/shard_map/all_to_all | solution.py:142
  185.1 10.4 %copy.155 = bf16[32,8,32,512]{3,2,1,0:T(8,128)(2,1)} copy(bf16[32,8,32,512]{3,1,2,0:T(8,128)(2,1)} %bitcast.192) | data formatting | bytes 16777216
  195.5 55.8 %fusion.10 = f32[256,31,128]{0,2,1:T(8,128)S(1)} fusion(bf16[256,32,512]{2,1,0:T(8,128)(2,1)} %bitcast.322, bf16[]{:T(256)} %bitcast.95, bf16[]{:T(256)} %bitcast.94, bf16[]{:T(256)} %bitcast.93, bf16[]{:T(256)} %bitcast.92, bf16[]{:T(256)} %bitcast.91, bf16[]{:T(256)} %bitcast.90, bf16[]{:T(256)} %bitcast.89, bf16[]{:T(256)} %bitcast.88, bf16[]{:T(256)} %bitcast.87, ...), kind=kOutput, calls=%fused_computation.19 | convolution fusion | flops 1049362432 | bytes 12452480 | tf_op jit(solution)/shard_map/slice | solution.py:44
  251.4 48.0 %add_convert_fusion = bf16[256,32,128]{0,2,1:T(8,128)(2,1)} fusion(f32[256,31,128]{0,2,1:T(8,128)S(1)} %fusion.10, bf16[256,32,512]{2,1,0:T(8,128)(2,1)S(1)} %bitcast.323, bf16[]{:T(256)} %bitcast.95, bf16[]{:T(256)} %bitcast.94, bf16[]{:T(256)} %bitcast.93, bf16[]{:T(256)} %bitcast.92, bf16[]{:T(256)} %bitcast.91, bf16[]{:T(256)} %bitcast.90, ...), kind=kOutput, calls=%fused_computation.31 | convolution fusion | flops 1084948480 | bytes 14549632 | tf_op jit(solution)/shard_map/dot_general | solution.py:38
  299.4 10.9 %fusion.3 = f32[256,2048]{1,0:T(8,128)} fusion(bf16[256,4096]{0,1:T(8,128)(2,1)} %bitcast.327, bf16[4096,1024]{1,0:T(8,128)(2,1)} %get-tuple-element.87, bf16[4096,1024]{1,0:T(8,128)(2,1)S(1)} %bitcast.321), kind=kOutput, calls=%fused_computation.10 | convolution fusion | flops 4328521728 | bytes 20971520 | tf_op jit(solution)/shard_map/dot_general | solution.py:74
  310.3 5.5 %fusion.625 = (f32[256]{0:T(256)S(1)}, f32[256,1024]{1,0:T(8,128)S(1)}) fusion(f32[1024]{0:T(1024)S(1)} %convert_reduce_fusion, f32[256,2048]{1,0:T(8,128)} %fusion.3), kind=kOutput, calls=%fused_computation.721 | convolution fusion | flops 3227516672 | bytes 3150848 | tf_op jit(solution)/shard_map/dot_general | solution.py:80
  316.1 1.2 fusion.21
  318.1 57.0 %all-gather.3.cloned.1.call-done = bf16[1024,2048]{1,0:T(8,128)(2,1)} async-done(((bf16[256,2048]{1,0:T(8,128)(2,1)}), bf16[1024,2048]{1,0:T(8,128)(2,1)}) %all-gather.3.cloned.1.call-update) | async-done | bytes 4194320 | tf_op jit(solution)/shard_map/all_gather | solution.py:162
  375.0 17.2 %while.2 = (s32[]{:T(128)}, bf16[1024,1,2048]{2,0,1:T(8,128)(2,1)}, s32[8,3]{0,1:T(4,128)S(1)}, bf16[8,8,1,2048]{3,1,2,0:T(8,128)(2,1)S(1)}, s32[]{:T(128)}) while((s32[]{:T(128)}, bf16[1024,1,2048]{2,0,1:T(8,128)(2,1)}, s32[8,3]{0,1:T(4,128)S(1)}, bf16[8,8,1,2048]{3,1,2,0:T(8,128)(2,1)S(1)}, s32[]{:T(128)}) %tuple.139), condition=%wide.while_cond, body=%wide.while_body.sunk | while | flops 2 | bytes 65641 | solution.py:97
  375.9 1.5 bitcast_dynamic-update-slice_fusion.4
  378.0 1.5 bitcast_dynamic-update-slice_fusion.4
  380.2 1.5 bitcast_dynamic-update-slice_fusion.4
  382.3 1.5 bitcast_dynamic-update-slice_fusion.4
  384.4 1.5 bitcast_dynamic-update-slice_fusion.4
  386.5 1.5 bitcast_dynamic-update-slice_fusion.4
  388.7 1.5 bitcast_dynamic-update-slice_fusion.4
  390.8 1.5 bitcast_dynamic-update-slice_fusion.4
  392.7 17.0 %while.3 = (s32[]{:T(128)}, bf16[1024,1,2048]{2,0,1:T(8,128)(2,1)}, s32[8,3]{0,1:T(4,128)S(1)}, bf16[8,8,1,2048]{3,1,2,0:T(8,128)(2,1)S(1)}, s32[]{:T(128)}) while((s32[]{:T(128)}, bf16[1024,1,2048]{2,0,1:T(8,128)(2,1)}, s32[8,3]{0,1:T(4,128)S(1)}, bf16[8,8,1,2048]{3,1,2,0:T(8,128)(2,1)S(1)}, s32[]{:T(128)}) %tuple.140), condition=%wide.while_cond.1, body=%wide.while_body.1.sunk | while | flops 2 | bytes 65641 | solution.py:97
  393.3 1.5 bitcast_dynamic-update-slice_fusion.5
  395.5 1.5 bitcast_dynamic-update-slice_fusion.5
  397.6 1.5 bitcast_dynamic-update-slice_fusion.5
  399.7 1.5 bitcast_dynamic-update-slice_fusion.5
  401.9 1.5 bitcast_dynamic-update-slice_fusion.5
  404.0 1.5 bitcast_dynamic-update-slice_fusion.5
  406.1 1.5 bitcast_dynamic-update-slice_fusion.5
  408.2 1.5 bitcast_dynamic-update-slice_fusion.5
  410.7 2.6 maximum_multiply_fusion
  413.4 9.7 %cosine_multiply_fusion = (f32[1024,512]{1,0:T(8,128)S(1)}, f32[1024,512]{1,0:T(8,128)}) fusion(s32[512]{0:T(512)S(1)} %iota_add_fusion.1, s32[1024]{0:T(1024)S(1)} %iota_add_fusion), kind=kLoop, calls=%fused_computation.44 | loop fusion | flops 8912896 | bytes 4200448 | tf_op jit(solution)/shard_map/mul | solution.py:62
  423.1 72.8 %reduce-scatter.2.cloned.1.call-done = f32[2,8,2048]{2,1,0:T(8,128)} async-done(((f32[64,8,2048]{2,1,0:T(8,128)}), f32[2,8,2048]{2,1,0:T(8,128)}) %reduce-scatter.2.cloned.1.call-update) | async-done | bytes 131088 | tf_op jit(solution)/shard_map/reduce_scatter | solution.py:129
  495.9 3.8 fusion.26
  (102 shorter events, 33.8 us)
Async XLA Ops:
  6.5 14.1 %copy-start = (bf16[8,32,16384]{2,1,0:T(8,128)(2,1)S(1)}, bf16[8,32,16384]{2,1,0:T(8,128)(2,1)}, u32[]{:S(2)}) copy-start(bf16[8,32,16384]{2,1,0:T(8,128)(2,1)} %param.6) | copy-start | bytes 25165828
  63.9 8.0 %copy-start.2 = (f32[64]{0:T(128)S(1)}, f32[64]{0:T(128)}, u32[]{:S(2)}) copy-start(f32[64]{0:T(128)} %param.7) | copy-start | bytes 772
  63.9 121.2 %all-to-all-start = ((bf16[32,8,1,16384]{3,1,2,0:T(8,128)(2,1)}), bf16[32,8,1,16384]{3,1,2,0:T(8,128)(2,1)}, u32[]{:S(2)}, u32[]{:S(2)}) async-start(bf16[32,8,1,16384]{3,1,2,0:T(8,128)(2,1)} %fusion.30), calls=%async_computation | async-start | bytes 16777216 | tf_op jit(solution)/shard_map/all_to_all | solution.py:142
  71.6 303.4 %all-gather.3.cloned.1.call-start = ((), (), s32[]{:S(2)}) async-start(), calls=%async_computation.3 | async-start | bytes 5242880 | tf_op jit(solution)/shard_map/all_gather | solution.py:162
  195.5 55.8 %copy-start.1 = (bf16[32,8,32,512]{3,2,1,0:T(8,128)(2,1)S(1)}, bf16[32,8,32,512]{3,2,1,0:T(8,128)(2,1)}, u32[]{:S(2)}) copy-start(bf16[32,8,32,512]{3,2,1,0:T(8,128)(2,1)} %copy.155) | copy-start | bytes 25165828
  195.5 103.9 %slice-start = ((s8[8388608]{0:T(1024)(128)(4,1)}), s8[4194304]{0:T(1024)(128)(4,1)S(1)}, s32[]{:S(2)}) async-start(s8[8388608]{0:T(1024)(128)(4,1)} %bitcast.320), calls=%async_computation.4 | async-start | bytes 8388608
  251.4 48.1 %slice-start.1 = ((s8[8388608]{0:T(1024)(128)(4,1)}), s8[4194304]{0:T(1024)(128)(4,1)S(1)}, s32[]{:S(2)}) async-start(s8[8388608]{0:T(1024)(128)(4,1)} %bitcast.320), calls=%async_computation.5 | async-start | bytes 8388608
  310.3 5.8 %copy-start.3 = (f32[256,2048]{1,0:T(8,128)S(1)}, f32[256,2048]{1,0:T(8,128)}, u32[]{:S(2)}) copy-start(f32[256,2048]{1,0:T(8,128)} %fusion.3) | copy-start | bytes 6291460
  310.3 7.1 %copy-start.5 = (s32[16]{0:T(128)S(1)}, s32[16]{0:T(128)}, u32[]{:S(2)}) copy-start(s32[16]{0:T(128)} %param.9) | copy-start | bytes 196
  310.3 7.4 %copy-start.4 = (s32[16,2]{0,1:T(2,128)S(1)}, s32[16,2]{0,1:T(2,128)}, u32[]{:S(2)}) copy-start(s32[16,2]{0,1:T(2,128)} %param.8) | copy-start | bytes 388
  317.4 178.6 %reduce-scatter.2.cloned.1.call-start = ((), (), s32[]{:S(2)}) async-start(), calls=%async_computation.2 | async-start | bytes 4325376 | tf_op jit(solution)/shard_map/reduce_scatter | solution.py:129
Sparse Core Ops, SparseCore 0:
  317.5 57.5 all-gather.2
  413.5 82.3 reduce-scatter.1
